TPU v7x, 512 devices: a whole 4x8x8 slice. The times are simulated.
512 devices in a mesh: band: 32 (over x, y), seq: 16 (over z, core).
Axes of the slice: x: 4, y: 8, z: 8, core: 2. Of those that a mesh axis runs over, the one named last changes fastest.
Arguments:
- posteriors: bfloat16 [32, 262144], P(None, ('band', 'seq'))
- seed_mask: int32 [262144], P(('band', 'seq')), may hold values 0 or 1
- frame_perm: int32 [512, 512], P(('band', 'seq')), may hold values from 0 to 511, each once within a row
- lengths: int32 [256], replicated, may hold values from 1 to 4096, 262144 in all
- embeddings: bfloat16 [262144, 256], P(('band', 'seq')), may hold values from -12 to 12
- partners: int32 [2048, 32], P(('band', 'seq')), may hold values from 0 to 127, as said below
- levels: int32 [2048, 32], P(('band', 'seq')), may hold values from 1 to 8, as said below
Outputs:
- spread_labels: float32 [32, 262144], P(None, ('band', 'seq'))
Inputs may be any that keep to these rules, and one draw needn't show every extreme that they name: `partners`: within each seq index s, slot k pairs the 128 tiles mutually: if tile number a names b in slot k then b names a in slot k; no tile names itself. `levels`: two tiles paired in slot k carry the same level.
All inputs are finite; a program needn't handle non-finite values. No bound on the sum of `seed_mask` on one device may be relied on, other than what follows from the above.
Results may differ from a plain program's by a relative error of at most 0.007.
Values may be sent and summed in bfloat16 or wider, within the bound.
No kernel may reach another device: no remote copies, remote signals or barrier semaphores. Data moves between devices by JAX's collectives and lax.ppermute only.
A program may use at most 64 MiB of HBM per device.

v0:
```python
import math
import jax
import jax.numpy as jnp
from jax import lax
from jax.sharding import PartitionSpec as P

RADIUS = 64
ITERS = 3
decay_len = 16.0
spread_rate = 0.9


def with_halo(cells, sides, width):
    for axis, dim in sides:
        count = lax.axis_size(axis)
        ends = count - 1
        head = lax.slice_in_dim(cells, 0, width, axis=dim)
        tail = lax.slice_in_dim(cells, cells.shape[dim] - width, cells.shape[dim], axis=dim)
        cells = jnp.concatenate(
            [
                lax.ppermute(tail, axis, [(i, (i + 1) % count) for i in range(ends)]),
                cells,
                lax.ppermute(head, axis, [((i + 1) % count, i) for i in range(ends)]),
            ],
            axis=dim,
        )
    return cells


def total_over_devices(values):
    for axis in ("seq", "band"):
        count = lax.axis_size(axis)
        spread = jnp.broadcast_to(values[None], (count,) + values.shape)
        rows = lax.all_to_all(spread, axis, split_axis=0, concat_axis=0, tiled=True)
        values = jnp.sum(rows, axis=0)
    return values


def band_gather(block):
    count = lax.axis_size("band")
    spread = jnp.broadcast_to(block[None], (count,) + block.shape)
    return lax.all_to_all(spread, "band", split_axis=0, concat_axis=0, tiled=True)


def on_device(posteriors, seed_mask, frame_perm, lengths, embeddings, partners, levels):
    channels, frames = posteriors.shape
    band_count = lax.axis_size("band")
    groups = lax.axis_size("seq")
    tile_count = frames // 128
    seeded = posteriors * seed_mask.astype(jnp.bfloat16)[None, :]
    ordered = jnp.take(seeded, frame_perm[0], axis=1).reshape(
        channels, band_count, frames // band_count
    )
    arrived = lax.all_to_all(ordered, "band", split_axis=1, concat_axis=1, tiled=True)
    labels = arrived.reshape(channels, frames).astype(jnp.float32)
    device = lax.axis_index("band") * groups + lax.axis_index("seq")
    frame_total = frames * band_count * groups
    window = 128 + 2 * RADIUS
    global_at = device * frames - RADIUS + jnp.arange(frames + 2 * RADIUS, dtype=jnp.int32)
    utt_ends = jnp.cumsum(lengths)
    owner_seg = jnp.sum((utt_ends[None, :] <= global_at[:, None]).astype(jnp.int32), axis=1)
    inside = (global_at >= 0) & (global_at < frame_total)
    tile_off = (jnp.arange(tile_count, dtype=jnp.int32) * 128)[:, None, None]
    win_pos = tile_off + jnp.arange(window, dtype=jnp.int32)[None, :, None]
    row_pos = tile_off + RADIUS + jnp.arange(128, dtype=jnp.int32)[None, None, :]
    offset = jnp.abs(win_pos - row_pos)
    linked = (
        (offset >= 1)
        & (offset <= RADIUS)
        & (owner_seg[win_pos] == owner_seg[row_pos])
        & inside[win_pos]
    )
    band_tiles = jnp.where(
        linked, jnp.exp(-offset.astype(jnp.float32) / decay_len), jnp.float32(0.0)
    ).astype(jnp.bfloat16)
    near_degree = jnp.sum(band_tiles.astype(jnp.float32), axis=1).reshape(frames)
    gathered = lax.all_gather(embeddings, "band", axis=0, tiled=True)
    labels_band = band_gather(arrived.reshape(channels, frames))
    labels_band, gathered = lax.optimization_barrier((labels_band, gathered))
    embed_width = embeddings.shape[1]
    partner_rows = gathered.reshape(-1, 128, embed_width)[partners]
    own_rows = embeddings.reshape(tile_count, 128, embed_width)
    inner_prod = jnp.einsum(
        "tkje,tie->tkji", partner_rows, own_rows, preferred_element_type=jnp.float32
    )
    affinity = (
        jnp.exp(0.5 * (inner_prod / math.sqrt(embed_width)))
        * (levels.astype(jnp.float32) / 8.0)[:, :, None, None]
        / 128.0
    )
    affinity = affinity.astype(jnp.bfloat16)
    far_degree = jnp.sum(affinity.astype(jnp.float32), axis=(1, 2)).reshape(frames)
    norm_scale = 1.0 / jnp.sqrt(near_degree + far_degree)

    def squares(residual):
        return total_over_devices(jnp.sum(residual * residual, axis=1))

    solution = jnp.zeros((channels, frames), jnp.float32)
    residual = labels
    direction = labels
    first_norm = jnp.sum(residual * residual, axis=1)
    scale_band = band_gather(norm_scale)
    for iteration in range(ITERS):
        lifted = (norm_scale[None, :] * direction).astype(jnp.bfloat16)
        padded = with_halo(lifted, ((("band", "seq"), 1),), RADIUS)
        windows = jnp.stack(
            [padded[:, position * 128 : position * 128 + window] for position in range(tile_count)],
            axis=0,
        )
        near_term = jnp.einsum(
            "tcw,twa->cta", windows, band_tiles, preferred_element_type=jnp.float32
        ).reshape(channels, frames)
        if iteration == 0:
            lifted_band = (scale_band[:, None, :] * labels_band.astype(jnp.float32)).astype(
                jnp.bfloat16
            )
        else:
            lifted_band = band_gather(lifted)
        spread = jnp.transpose(lifted_band, (1, 0, 2)).reshape(channels, -1, 128)
        far_tiles = spread[:, partners]
        far_term = jnp.einsum(
            "ctkj,tkji->cti", far_tiles, affinity, preferred_element_type=jnp.float32
        ).reshape(channels, frames)
        image = direction - spread_rate * norm_scale[None, :] * (near_term + far_term)
        sums = [jnp.sum(direction * image, axis=1)]
        last = iteration == ITERS - 1
        if not last:
            sums += [jnp.sum(residual * image, axis=1), jnp.sum(image * image, axis=1)]
        if iteration == 0:
            sums.append(first_norm)
        totals = total_over_devices(jnp.stack(sums))
        curve = totals[0]
        if iteration == 0:
            norm_now = totals[-1]
        alpha = norm_now / curve
        solution = solution + alpha[:, None] * direction
        if not last:
            residual = residual - alpha[:, None] * image
            norm_next = norm_now - 2.0 * alpha * totals[1] + alpha * alpha * totals[2]
            direction = residual + (norm_next / norm_now)[:, None] * direction
            norm_now = norm_next
    return solution


def solution(mesh):
    placed = (
        P(None, ("band", "seq")),
        P(("band", "seq")),
        P(("band", "seq"), None),
        P(),
        P(("band", "seq"), None),
        P(("band", "seq"), None),
        P(("band", "seq"), None),
    )
    return jax.shard_map(
        on_device, mesh=mesh, in_specs=placed, out_specs=P(None, ("band", "seq")), check_vma=False
    )
```

profile of v0, /device:TPU:1, one launch (start us, length us, event | category | flops | bytes accessed | tf_op | source)
XLA Modules:
  0.0 341.7 jit_solution(14593774616092935248)
XLA Ops:
  13.7 10.5 %all-to-all-start = ((bf16[32,2,256]{2,1,0:T(2,128)(2,1)}), bf16[32,2,256]{2,1,0:T(2,128)(2,1)S(1)}, u32[]{:S(2)}, u32[]{:S(2)}) async-start(bf16[32,2,256]{2,1,0:T(2,128)(2,1)} %reshape.829), calls=%async_computation | async-start | bytes 65536 | tf_op jit(solution)/shard_map/all_to_all | solution.py:54
  25.6 7.4 %all-to-all-done = bf16[32,2,256]{2,1,0:T(2,128)(2,1)S(1)} async-done(((bf16[32,2,256]{2,1,0:T(2,128)(2,1)}), bf16[32,2,256]{2,1,0:T(2,128)(2,1)S(1)}, u32[]{:S(2)}, u32[]{:S(2)}) %all-to-all-start) | async-done | bytes 32800 | tf_op jit(solution)/shard_map/all_to_all | solution.py:54
  34.4 3.9 %all-to-all-start.1 = ((bf16[32,32,512]{2,1,0:T(8,128)(2,1)}), bf16[32,32,512]{2,1,0:T(8,128)(2,1)S(1)}, u32[]{:S(2)}, u32[]{:S(2)}) async-start(bf16[32,32,512]{2,1,0:T(8,128)(2,1)} %broadcast_in_dim.40), calls=%async_computation.1 | async-start | bytes 2097152 | tf_op jit(solution)/shard_map/all_to_all | solution.py:42
  38.7 4.5 %gather_fusion.1 = s32[1024]{0:T(1024)S(1)} fusion(s32[640]{0:T(1024)S(1)} %convert_reduce_fusion.1, s32[1024]{0:T(1024)S(1)} %broadcast_clamp_fusion), kind=kCustom, calls=%fused_computation.1 | custom fusion | bytes 12288 | tf_op jit(solution)/shard_map/gather | solution.py:70
  45.6 6.8 %gather_fusion.3 = pred[1024]{0:T(1024)(128)(4,1)S(1)} fusion(pred[640]{0:T(1024)(128)(4,1)S(1)} %compare_and_fusion.1, s32[1024]{0:T(1024)S(1)} %broadcast_clamp_fusion), kind=kCustom, calls=%fused_computation.3 | custom fusion | bytes 6144 | tf_op jit(solution)/shard_map/gather | solution.py:71
  53.3 16.7 %all-to-all-done.1 = bf16[32,32,512]{2,1,0:T(8,128)(2,1)S(1)} async-done(((bf16[32,32,512]{2,1,0:T(8,128)(2,1)}), bf16[32,32,512]{2,1,0:T(8,128)(2,1)S(1)}, u32[]{:S(2)}, u32[]{:S(2)}) %all-to-all-start.1) | async-done | bytes 1048608 | tf_op jit(solution)/shard_map/all_to_all | solution.py:42
  70.0 58.1 %all-gather.2.cloned.1.call-done = bf16[16384,256]{1,0:T(8,128)(2,1)} async-done(((bf16[512,256]{1,0:T(8,128)(2,1)}), bf16[16384,256]{1,0:T(8,128)(2,1)}) %all-gather.2.cloned.1.call-update) | async-done | bytes 8388624 | tf_op jit(solution)/shard_map/all_gather | solution.py:77
  128.2 10.0 %gather_fusion.4 = bf16[128,128,256]{2,1,0:T(8,128)(2,1)} fusion(bf16[128,128,256]{2,1,0:T(8,128)(2,1)} %bitcast.181, s32[1024]{0:T(1024)S(1)} %pad_clamp_fusion), kind=kCustom, calls=%fused_computation.4 | custom fusion | bytes 16777728 | tf_op jit(solution)/shard_map/gather | solution.py:81
  138.1 7.7 %convert_reduce_fusion = (f32[4,128]{1,0:T(4,128)S(1)}, bf16[4,32,128,128]{3,2,1,0:T(8,128)(2,1)}) fusion(f32[4,32]{1,0:T(4,128)S(1)} %convert_multiply_fusion.6, bf16[4,32,128,256]{3,2,1,0:T(8,128)(2,1)} %bitcast.182, bf16[4,128,256,1]{2,1,3,0:T(8,128)(2,1)S(1)} %bitcast.198), kind=kOutput, calls=%fused_computation.8 | convolution fusion | flops 1086324224 | bytes 12847616 | tf_op jit(solution)/shard_map/tkje,tie->tkji/dot_general | solution.py:83
  145.9 4.2 %collective-permute-start = (bf16[32,64]{1,0:T(8,128)(2,1)S(1)}, bf16[32,64]{1,0:T(8,128)(2,1)S(1)}, u32[]{:S(2)}, u32[]{:S(2)}) collective-permute-start(bf16[32,64]{1,0:T(8,128)(2,1)S(1)} %get-tuple-element.41), channel_id=1, source_target_pairs={{0,1},{1,2},{2,3},{3,4},{4,5},{5,6},{6,7},{7,8},{8,9},{9,10},{10,1... | collective-permute-start | bytes 12296 | tf_op jit(solution)/shard_map/ppermute | solution.py:21
  152.8 5.7 %all-to-all-start.2 = ((f32[32,1,512]{2,1,0:T(1,128)}), f32[32,1,512]{2,1,0:T(1,128)S(1)}, u32[]{:S(2)}, u32[]{:S(2)}) async-start(f32[32,1,512]{2,1,0:T(1,128)} %mul.397), calls=%async_computation.2 | async-start | bytes 131072 | tf_op jit(solution)/shard_map/all_to_all | solution.py:42
  159.2 7.9 %all-to-all-done.2 = f32[32,1,512]{2,1,0:T(1,128)S(1)} async-done(((f32[32,1,512]{2,1,0:T(1,128)}), f32[32,1,512]{2,1,0:T(1,128)S(1)}, u32[]{:S(2)}, u32[]{:S(2)}) %all-to-all-start.2) | async-done | bytes 65568 | tf_op jit(solution)/shard_map/all_to_all | solution.py:42
  173.5 17.3 %all_to_all.56 = f32[16,1,128]{2,1,0:T(1,128)S(1)} all-to-all(f32[16,1,128]{2,1,0:T(1,128)S(1)} %reshape.831), channel_id=1, replica_groups=mesh['band'=32,'seq'=16] {'seq'}, dimensions={0} | all-to-all | bytes 16384 | tf_op jit(solution)/shard_map/all_to_all | solution.py:34
  192.2 11.6 %all_to_all.57 = f32[32,1,128]{2,1,0:T(1,128)S(1)} all-to-all(f32[32,1,128]{2,1,0:T(1,128)S(1)} %reshape.833), channel_id=1, replica_groups=mesh['band'=32,'seq'=16] {'band'}, dimensions={0} | all-to-all | bytes 32768 | tf_op jit(solution)/shard_map/all_to_all | solution.py:34
  205.9 3.9 %all-to-all-start.5 = ((bf16[32,32,512]{2,1,0:T(8,128)(2,1)}), bf16[32,32,512]{2,1,0:T(8,128)(2,1)S(1)}, u32[]{:S(2)}, u32[]{:S(2)}) async-start(bf16[32,32,512]{2,1,0:T(8,128)(2,1)} %broadcast_in_dim.44), calls=%async_computation.5 | async-start | bytes 2097152 | tf_op jit(solution)/shard_map/all_to_all | solution.py:42
  209.9 4.0 %collective-permute-start.2 = (bf16[32,64]{1,0:T(8,128)(2,1)S(1)}, bf16[32,64]{1,0:T(8,128)(2,1)S(1)}, u32[]{:S(2)}, u32[]{:S(2)}) collective-permute-start(bf16[32,64]{1,0:T(8,128)(2,1)S(1)} %get-tuple-element.35), channel_id=1, source_target_pairs={{0,1},{1,2},{2,3},{3,4},{4,5},{5,6},{6,7},{7,8},{8,9},{9,10},{10,1... | collective-permute-start | bytes 12296 | tf_op jit(solution)/shard_map/ppermute | solution.py:21
  219.9 14.5 %all-to-all-done.5 = bf16[32,32,512]{2,1,0:T(8,128)(2,1)S(1)} async-done(((bf16[32,32,512]{2,1,0:T(8,128)(2,1)}), bf16[32,32,512]{2,1,0:T(8,128)(2,1)S(1)}, u32[]{:S(2)}, u32[]{:S(2)}) %all-to-all-start.5) | async-done | bytes 1048608 | tf_op jit(solution)/shard_map/all_to_all | solution.py:42
  240.4 15.1 %all_to_all.58 = f32[16,3,32]{2,1,0:T(4,128)S(1)} all-to-all(f32[16,3,32]{2,1,0:T(4,128)S(1)} %broadcast_in_dim.45), channel_id=1, replica_groups=mesh['band'=32,'seq'=16] {'seq'}, dimensions={0} | all-to-all | bytes 12288 | tf_op jit(solution)/shard_map/all_to_all | solution.py:34
  255.5 14.1 %all_to_all.59 = f32[32,3,32]{2,1,0:T(4,128)S(1)} all-to-all(f32[32,3,32]{2,1,0:T(4,128)S(1)} %broadcast_in_dim.46), channel_id=1, replica_groups=mesh['band'=32,'seq'=16] {'band'}, dimensions={0} | all-to-all | bytes 24576 | tf_op jit(solution)/shard_map/all_to_all | solution.py:34
  270.9 3.9 %all-to-all-start.8 = ((bf16[32,32,512]{2,1,0:T(8,128)(2,1)}), bf16[32,32,512]{2,1,0:T(8,128)(2,1)S(1)}, u32[]{:S(2)}, u32[]{:S(2)}) async-start(bf16[32,32,512]{2,1,0:T(8,128)(2,1)} %broadcast_in_dim.47), calls=%async_computation.8 | async-start | bytes 2097152 | tf_op jit(solution)/shard_map/all_to_all | solution.py:42
  274.9 3.9 %collective-permute-start.4 = (bf16[32,64]{1,0:T(8,128)(2,1)S(1)}, bf16[32,64]{1,0:T(8,128)(2,1)S(1)}, u32[]{:S(2)}, u32[]{:S(2)}) collective-permute-start(bf16[32,64]{1,0:T(8,128)(2,1)S(1)} %get-tuple-element.29), channel_id=1, source_target_pairs={{0,1},{1,2},{2,3},{3,4},{4,5},{5,6},{6,7},{7,8},{8,9},{9,10},{10,1... | collective-permute-start | bytes 12296 | tf_op jit(solution)/shard_map/ppermute | solution.py:21
  284.7 14.7 %all-to-all-done.8 = bf16[32,32,512]{2,1,0:T(8,128)(2,1)S(1)} async-done(((bf16[32,32,512]{2,1,0:T(8,128)(2,1)}), bf16[32,32,512]{2,1,0:T(8,128)(2,1)S(1)}, u32[]{:S(2)}, u32[]{:S(2)}) %all-to-all-start.8) | async-done | bytes 1048608 | tf_op jit(solution)/shard_map/all_to_all | solution.py:42
  305.5 14.7 %all_to_all.60 = f32[16,1,32]{2,1,0:T(1,128)S(1)} all-to-all(f32[16,1,32]{2,1,0:T(1,128)S(1)} %broadcast_in_dim.48), channel_id=1, replica_groups=mesh['band'=32,'seq'=16] {'seq'}, dimensions={0} | all-to-all | bytes 4096 | tf_op jit(solution)/shard_map/all_to_all | solution.py:34
  320.2 13.9 %all_to_all.61 = f32[32,1,32]{2,1,0:T(1,128)S(1)} all-to-all(f32[32,1,32]{2,1,0:T(1,128)S(1)} %broadcast_in_dim.49), channel_id=1, replica_groups=mesh['band'=32,'seq'=16] {'band'}, dimensions={0} | all-to-all | bytes 8192 | tf_op jit(solution)/shard_map/all_to_all | solution.py:34
  (123 shorter events, 52.7 us)
Async XLA Ops:
  6.5 45.9 %copy-start.1 = (s32[4,32]{1,0:T(4,128)S(1)}, s32[4,32]{1,0:T(4,128)}, u32[]{:S(2)}) copy-start(s32[4,32]{1,0:T(4,128)} %param.12) | copy-start | bytes 1540
  6.5 46.7 %copy-start.2 = (s32[4,32]{1,0:T(4,128)S(1)}, s32[4,32]{1,0:T(4,128)}, u32[]{:S(2)}) copy-start(s32[4,32]{1,0:T(4,128)} %param.13) | copy-start | bytes 1540
  6.5 121.6 %all-gather.2.cloned.1.call-start = ((), (), s32[]{:S(2)}) async-start(), calls=%async_computation.11 | async-start | bytes 8650752 | tf_op jit(solution)/shard_map/all_gather | solution.py:77
  13.7 19.3 %all-to-all-start = ((bf16[32,2,256]{2,1,0:T(2,128)(2,1)}), bf16[32,2,256]{2,1,0:T(2,128)(2,1)S(1)}, u32[]{:S(2)}, u32[]{:S(2)}) async-start(bf16[32,2,256]{2,1,0:T(2,128)(2,1)} %reshape.829), calls=%async_computation | async-start | bytes 65536 | tf_op jit(solution)/shard_map/all_to_all | solution.py:54
  34.4 35.6 %all-to-all-start.1 = ((bf16[32,32,512]{2,1,0:T(8,128)(2,1)}), bf16[32,32,512]{2,1,0:T(8,128)(2,1)S(1)}, u32[]{:S(2)}, u32[]{:S(2)}) async-start(bf16[32,32,512]{2,1,0:T(8,128)(2,1)} %broadcast_in_dim.40), calls=%async_computation.1 | async-start | bytes 2097152 | tf_op jit(solution)/shard_map/all_to_all | solution.py:42
  128.1 10.0 %copy-start = (bf16[512,256]{1,0:T(8,128)(2,1)S(1)}, bf16[512,256]{1,0:T(8,128)(2,1)}, u32[]{:S(2)}) copy-start(bf16[512,256]{1,0:T(8,128)(2,1)} %param.11) | copy-start | bytes 786436
  145.9 12.6 %collective-permute-start = (bf16[32,64]{1,0:T(8,128)(2,1)S(1)}, bf16[32,64]{1,0:T(8,128)(2,1)S(1)}, u32[]{:S(2)}, u32[]{:S(2)}) collective-permute-start(bf16[32,64]{1,0:T(8,128)(2,1)S(1)} %get-tuple-element.41), channel_id=1, source_target_pairs={{0,1},{1,2},{2,3},{3,4},{4,5},{5,6},{6,7},{7,8},{8,9},{9,10},{10,1... | collective-permute-start | bytes 12296 | tf_op jit(solution)/shard_map/ppermute | solution.py:21
  150.2 8.4 %collective-permute-start.1 = (bf16[32,64]{1,0:T(8,128)(2,1)S(1)}, bf16[32,64]{1,0:T(8,128)(2,1)S(1)}, u32[]{:S(2)}, u32[]{:S(2)}) collective-permute-start(bf16[32,64]{1,0:T(8,128)(2,1)S(1)} %get-tuple-element.42), channel_id=1, source_target_pairs={{1,0},{2,1},{3,2},{4,3},{5,4},{6,5},{7,6},{8,7},{9,8},{10,9},{11,1... | collective-permute-start | bytes 12296 | tf_op jit(solution)/shard_map/ppermute | solution.py:23
  152.8 14.4 %all-to-all-start.2 = ((f32[32,1,512]{2,1,0:T(1,128)}), f32[32,1,512]{2,1,0:T(1,128)S(1)}, u32[]{:S(2)}, u32[]{:S(2)}) async-start(f32[32,1,512]{2,1,0:T(1,128)} %mul.397), calls=%async_computation.2 | async-start | bytes 131072 | tf_op jit(solution)/shard_map/all_to_all | solution.py:42
  205.9 28.5 %all-to-all-start.5 = ((bf16[32,32,512]{2,1,0:T(8,128)(2,1)}), bf16[32,32,512]{2,1,0:T(8,128)(2,1)S(1)}, u32[]{:S(2)}, u32[]{:S(2)}) async-start(bf16[32,32,512]{2,1,0:T(8,128)(2,1)} %broadcast_in_dim.44), calls=%async_computation.5 | async-start | bytes 2097152 | tf_op jit(solution)/shard_map/all_to_all | solution.py:42
  209.9 6.0 %collective-permute-start.2 = (bf16[32,64]{1,0:T(8,128)(2,1)S(1)}, bf16[32,64]{1,0:T(8,128)(2,1)S(1)}, u32[]{:S(2)}, u32[]{:S(2)}) collective-permute-start(bf16[32,64]{1,0:T(8,128)(2,1)S(1)} %get-tuple-element.35), channel_id=1, source_target_pairs={{0,1},{1,2},{2,3},{3,4},{4,5},{5,6},{6,7},{7,8},{8,9},{9,10},{10,1... | collective-permute-start | bytes 12296 | tf_op jit(solution)/shard_map/ppermute | solution.py:21
  213.9 5.3 %collective-permute-start.3 = (bf16[32,64]{1,0:T(8,128)(2,1)S(1)}, bf16[32,64]{1,0:T(8,128)(2,1)S(1)}, u32[]{:S(2)}, u32[]{:S(2)}) collective-permute-start(bf16[32,64]{1,0:T(8,128)(2,1)S(1)} %get-tuple-element.36), channel_id=1, source_target_pairs={{1,0},{2,1},{3,2},{4,3},{5,4},{6,5},{7,6},{8,7},{9,8},{10,9},{11,1... | collective-permute-start | bytes 12296 | tf_op jit(solution)/shard_map/ppermute | solution.py:23
  270.9 28.5 %all-to-all-start.8 = ((bf16[32,32,512]{2,1,0:T(8,128)(2,1)}), bf16[32,32,512]{2,1,0:T(8,128)(2,1)S(1)}, u32[]{:S(2)}, u32[]{:S(2)}) async-start(bf16[32,32,512]{2,1,0:T(8,128)(2,1)} %broadcast_in_dim.47), calls=%async_computation.8 | async-start | bytes 2097152 | tf_op jit(solution)/shard_map/all_to_all | solution.py:42
  274.9 6.0 %collective-permute-start.4 = (bf16[32,64]{1,0:T(8,128)(2,1)S(1)}, bf16[32,64]{1,0:T(8,128)(2,1)S(1)}, u32[]{:S(2)}, u32[]{:S(2)}) collective-permute-start(bf16[32,64]{1,0:T(8,128)(2,1)S(1)} %get-tuple-element.29), channel_id=1, source_target_pairs={{0,1},{1,2},{2,3},{3,4},{4,5},{5,6},{6,7},{7,8},{8,9},{9,10},{10,1... | collective-permute-start | bytes 12296 | tf_op jit(solution)/shard_map/ppermute | solution.py:21
  278.8 5.3 %collective-permute-start.5 = (bf16[32,64]{1,0:T(8,128)(2,1)S(1)}, bf16[32,64]{1,0:T(8,128)(2,1)S(1)}, u32[]{:S(2)}, u32[]{:S(2)}) collective-permute-start(bf16[32,64]{1,0:T(8,128)(2,1)S(1)} %get-tuple-element.30), channel_id=1, source_target_pairs={{1,0},{2,1},{3,2},{4,3},{5,4},{6,5},{7,6},{8,7},{9,8},{10,9},{11,1... | collective-permute-start | bytes 12296 | tf_op jit(solution)/shard_map/ppermute | solution.py:23
Sparse Core Ops, SparseCore 0:
  10.5 117.5 all-gather.1
where the time goes:
time: 343 us; the launch traced here: 342 us
  waiting for transfers between devices  126 us (37%)
  blocking collectives  86.7 us (25%)
  starting transfers between devices  46.1 us (13%)
  local copies, waits for them, and re-layouts  40.7 us (12%)
  matrix products  18.3 us (5%)
  between operations  13.9 us (4%)
  other arithmetic  9.58 us (3%)
    all_to_all x6, blocking collectives, total_over_devices(): rows = lax.all_to_all(spread, axis, split_axis=0, concat_axis=0, tiled=True)  86.7 us
    all_gather x1, waiting for transfers between devices, on_device(): gathered = lax.all_gather(embeddings, 'band', axis=0, tiled=True)  58.1 us
    all_to_all x4, waiting for transfers between devices, band_gather(): lax.all_to_all(spread, 'band', split_axis=0, concat_axis=0, tiled=True)  53.8 us
    all_to_all x4, starting transfers between devices, band_gather(): lax.all_to_all(spread, 'band', split_axis=0, concat_axis=0, tiled=True)  17.5 us
    ppermute x3, starting transfers between devices, with_halo(): lax.ppermute(tail, axis, [(i, (i + 1) % count) for i in range(ends)])  12.1 us
    all_to_all x1, starting transfers between devices, on_device(): lax.all_to_all(ordered, 'band', split_axis=1, concat_axis=1, tiled=True)  10.5 us
    gather x1, local copies, waits for them, and re-layouts, on_device(): partner_rows = gathered.reshape(-1, 128, embed_width)[partners]  9.99 us
    dot_general x3, matrix products, on_device(): jnp.einsum('ctkj,tkji->cti', far_tiles, affinity, preferred_element_type=...  8.82 us
  transfers between devices with their start and end apart: 12, of which 8 were waited for; matrix products, arithmetic and copies ran while one was open for 8% of the time, Pallas kernels for 0%

commit v1 on v0

--- a/solution.py
+++ b/solution.py
@@ -74,7 +74,9 @@
         linked, jnp.exp(-offset.astype(jnp.float32) / decay_len), jnp.float32(0.0)
     ).astype(jnp.bfloat16)
     near_degree = jnp.sum(band_tiles.astype(jnp.float32), axis=1).reshape(frames)
-    gathered = lax.all_gather(embeddings, "band", axis=0, tiled=True)
+    gathered = jnp.concatenate(
+        lax.all_to_all(jnp.stack([embeddings] * lax.axis_size("band")), "band", 0, 0), axis=0
+    )
     labels_band = band_gather(arrived.reshape(channels, frames))
     labels_band, gathered = lax.optimization_barrier((labels_band, gathered))
     embed_width = embeddings.shape[1]

time: 343 us -> 468 us (1.36)
  waiting for transfers between devices: 126 us -> 212 us
  blocking collectives: 86.7 us -> 135 us
  between operations: 13.9 us -> 0.52 us
    all_to_all x1, waiting for transfers between devices: 7.39 us -> 168 us  [on_device(): lax.all_to_all(jnp.stack([embeddings] * lax.axis_size('band')), 'band', 0...]
    all_gather x1 -> x0, waiting for transfers between devices: 58.1 us -> none  [on_device(): gathered = lax.all_gather(embeddings, 'band', axis=0, tiled=True)]
    all_to_all x0 -> x2, blocking collectives: none -> 46.5 us  [the longest x1 27.4 us: band_gather(): lax.all_to_all(spread, 'band', split_axis=0, concat_axis=0, tiled=True)]
    all_to_all x4 -> x3, waiting for transfers between devices: 53.8 us -> 37.1 us  [band_gather(): lax.all_to_all(spread, 'band', split_axis=0, concat_axis=0, tiled=True)]
    another operation x1 -> x2, local copies, waits for them, and re-layouts: 0.11 us -> 5.22 us  [the longest x1 5.1 us: on_device(): jnp.stack([embeddings] * lax.axis_size('band'))]
    all_to_all x4 -> x3, starting transfers between devices: 17.5 us -> 19.5 us  [band_gather(): lax.all_to_all(spread, 'band', split_axis=0, concat_axis=0, tiled=True)]
  transfers between devices with their start and end apart: 12 -> 10, of which waited for: 8 -> 6; matrix products, arithmetic and copies ran while one was open for 8% -> 4% of each run, Pallas kernels for 0% -> 0%
where the time goes in v1:
time: 468 us; the launch traced here: 467 us
  waiting for transfers between devices  212 us (45%)
  blocking collectives  135 us (29%)
  starting transfers between devices  48 us (10%)
  local copies, waits for them, and re-layouts  44.1 us (9%)
  matrix products  18.2 us (4%)
  other arithmetic  8.91 us (2%)
    all_to_all x1, waiting for transfers between devices, on_device(): lax.all_to_all(jnp.stack([embeddings] * lax.axis_size('band')), 'band', 0...  168 us
    all_to_all x6, blocking collectives, total_over_devices(): rows = lax.all_to_all(spread, axis, split_axis=0, concat_axis=0, tiled=True)  88.9 us
    all_to_all x3, waiting for transfers between devices, band_gather(): lax.all_to_all(spread, 'band', split_axis=0, concat_axis=0, tiled=True)  37.1 us
    all_to_all x1, blocking collectives, band_gather(): lax.all_to_all(spread, 'band', split_axis=0, concat_axis=0, tiled=True)  27.4 us
    all_to_all x3, starting transfers between devices, band_gather(): lax.all_to_all(spread, 'band', split_axis=0, concat_axis=0, tiled=True)  19.5 us
    all_to_all x1, blocking collectives, on_device(): lax.all_to_all(ordered, 'band', split_axis=1, concat_axis=1, tiled=True)  19.1 us
    ppermute x3, starting transfers between devices, with_halo(): lax.ppermute(tail, axis, [(i, (i + 1) % count) for i in range(ends)])  14 us
    gather x1, local copies, waits for them, and re-layouts, on_device(): partner_rows = gathered.reshape(-1, 128, embed_width)[partners]  9.99 us
  transfers between devices with their start and end apart: 10, of which 6 were waited for; matrix products, arithmetic and copies ran while one was open for 4% of the time, Pallas kernels for 0%

profile of v1, /device:TPU:1, one launch (start us, length us, event | category | flops | bytes accessed | tf_op | source)
XLA Modules:
  0.0 466.6 jit_solution(6822581995133506168)
XLA Ops:
  5.9 19.1 %all_to_all.61 = bf16[32,2,256]{2,1,0:T(2,128)(2,1)S(1)} all-to-all(bf16[32,2,256]{2,1,0:T(2,128)(2,1)S(1)} %reshape.835), channel_id=1, replica_groups=mesh['band'=32,'seq'=16] {'band'}, dimensions={0} | all-to-all | bytes 65536 | tf_op jit(solution)/shard_map/all_to_all | solution.py:54
  25.3 27.4 %all_to_all.62 = bf16[32,32,512]{2,1,0:T(8,128)(2,1)S(1)} all-to-all(bf16[32,32,512]{2,1,0:T(8,128)(2,1)S(1)} %broadcast_in_dim.40), channel_id=1, replica_groups=mesh['band'=32,'seq'=16] {'band'}, dimensions={0} | all-to-all | bytes 2097152 | tf_op jit(solution)/shard_map/all_to_all | solution.py:42
  52.7 5.1 %stack.48 = bf16[32,512,256]{2,1,0:T(8,128)(2,1)} broadcast(bf16[512,256]{1,0:T(8,128)(2,1)} %param.11), dimensions={1,2} | broadcast | bytes 8650752 | tf_op jit(solution)/shard_map/stack | solution.py:78
  57.8 8.5 %all-to-all-start.2 = ((bf16[32,512,256]{2,1,0:T(8,128)(2,1)}), bf16[32,512,256]{2,1,0:T(8,128)(2,1)}, u32[]{:S(2)}, u32[]{:S(2)}) async-start(bf16[32,512,256]{2,1,0:T(8,128)(2,1)} %stack.48), calls=%async_computation.2 | async-start | bytes 16777216 | tf_op jit(solution)/shard_map/all_to_all | solution.py:78
  67.3 4.5 gather_fusion.1
  74.2 6.8 %gather_fusion.3 = pred[1024]{0:T(1024)(128)(4,1)S(1)} fusion(pred[640]{0:T(1024)(128)(4,1)S(1)} %compare_and_fusion.1, s32[1024]{0:T(1024)S(1)} %broadcast_clamp_fusion), kind=kCustom, calls=%fused_computation.3 | custom fusion | bytes 6144 | tf_op jit(solution)/shard_map/gather | solution.py:71
  81.9 168.1 %all-to-all-done.2 = bf16[32,512,256]{2,1,0:T(8,128)(2,1)} async-done(((bf16[32,512,256]{2,1,0:T(8,128)(2,1)}), bf16[32,512,256]{2,1,0:T(8,128)(2,1)}, u32[]{:S(2)}, u32[]{:S(2)}) %all-to-all-start.2) | async-done | bytes 8388640 | tf_op jit(solution)/shard_map/all_to_all | solution.py:78
  250.0 10.0 %gather_fusion.4 = bf16[128,128,256]{2,1,0:T(8,128)(2,1)} fusion(bf16[128,128,256]{2,1,0:T(8,128)(2,1)} %bitcast.10, s32[1024]{0:T(1024)S(1)} %pad_clamp_fusion), kind=kCustom, calls=%fused_computation.4 | custom fusion | bytes 16777728 | tf_op jit(solution)/shard_map/gather | solution.py:83
  259.9 7.7 %convert_reduce_fusion = (f32[4,128]{1,0:T(4,128)S(1)}, bf16[4,32,128,128]{3,2,1,0:T(8,128)(2,1)}) fusion(f32[4,32]{1,0:T(4,128)S(1)} %convert_multiply_fusion.6, bf16[4,32,128,256]{3,2,1,0:T(8,128)(2,1)} %bitcast.182, bf16[4,128,256,1]{2,1,3,0:T(8,128)(2,1)S(1)} %bitcast.197), kind=kOutput, calls=%fused_computation.8 | convolution fusion | flops 1086324224 | bytes 12847616 | tf_op jit(solution)/shard_map/tkje,tie->tkji/dot_general | solution.py:85
  267.7 6.1 %collective-permute-start = (bf16[32,64]{1,0:T(8,128)(2,1)S(1)}, bf16[32,64]{1,0:T(8,128)(2,1)S(1)}, u32[]{:S(2)}, u32[]{:S(2)}) collective-permute-start(bf16[32,64]{1,0:T(8,128)(2,1)S(1)} %get-tuple-element.41), channel_id=1, source_target_pairs={{0,1},{1,2},{2,3},{3,4},{4,5},{5,6},{6,7},{7,8},{8,9},{9,10},{10,1... | collective-permute-start | bytes 12296 | tf_op jit(solution)/shard_map/ppermute | solution.py:21
  276.5 11.6 %all-to-all-start.3 = ((f32[32,1,512]{2,1,0:T(1,128)}), f32[32,1,512]{2,1,0:T(1,128)S(1)}, u32[]{:S(2)}, u32[]{:S(2)}) async-start(f32[32,1,512]{2,1,0:T(1,128)} %mul.397), calls=%async_computation.3 | async-start | bytes 131072 | tf_op jit(solution)/shard_map/all_to_all | solution.py:42
  288.9 7.9 %all-to-all-done.3 = f32[32,1,512]{2,1,0:T(1,128)S(1)} async-done(((f32[32,1,512]{2,1,0:T(1,128)}), f32[32,1,512]{2,1,0:T(1,128)S(1)}, u32[]{:S(2)}, u32[]{:S(2)}) %all-to-all-start.3) | async-done | bytes 65568 | tf_op jit(solution)/shard_map/all_to_all | solution.py:42
  303.1 19.5 %all_to_all.63 = f32[16,1,128]{2,1,0:T(1,128)S(1)} all-to-all(f32[16,1,128]{2,1,0:T(1,128)S(1)} %reshape.837), channel_id=1, replica_groups=mesh['band'=32,'seq'=16] {'seq'}, dimensions={0} | all-to-all | bytes 16384 | tf_op jit(solution)/shard_map/all_to_all | solution.py:34
  324.0 11.6 %all_to_all.64 = f32[32,1,128]{2,1,0:T(1,128)S(1)} all-to-all(f32[32,1,128]{2,1,0:T(1,128)S(1)} %reshape.839), channel_id=1, replica_groups=mesh['band'=32,'seq'=16] {'band'}, dimensions={0} | all-to-all | bytes 32768 | tf_op jit(solution)/shard_map/all_to_all | solution.py:34
  337.7 3.9 all-to-all-start.6
  341.7 4.0 collective-permute-start.2
  351.7 14.5 %all-to-all-done.6 = bf16[32,32,512]{2,1,0:T(8,128)(2,1)S(1)} async-done(((bf16[32,32,512]{2,1,0:T(8,128)(2,1)}), bf16[32,32,512]{2,1,0:T(8,128)(2,1)S(1)}, u32[]{:S(2)}, u32[]{:S(2)}) %all-to-all-start.6) | async-done | bytes 1048608 | tf_op jit(solution)/shard_map/all_to_all | solution.py:42
  372.2 15.1 %all_to_all.65 = f32[16,3,32]{2,1,0:T(4,128)S(1)} all-to-all(f32[16,3,32]{2,1,0:T(4,128)S(1)} %broadcast_in_dim.45), channel_id=1, replica_groups=mesh['band'=32,'seq'=16] {'seq'}, dimensions={0} | all-to-all | bytes 12288 | tf_op jit(solution)/shard_map/all_to_all | solution.py:34
  387.3 14.1 %all_to_all.66 = f32[32,3,32]{2,1,0:T(4,128)S(1)} all-to-all(f32[32,3,32]{2,1,0:T(4,128)S(1)} %broadcast_in_dim.46), channel_id=1, replica_groups=mesh['band'=32,'seq'=16] {'band'}, dimensions={0} | all-to-all | bytes 24576 | tf_op jit(solution)/shard_map/all_to_all | solution.py:34
  402.7 3.9 all-to-all-start.9
  406.7 3.9 collective-permute-start.4
  416.6 14.7 %all-to-all-done.9 = bf16[32,32,512]{2,1,0:T(8,128)(2,1)S(1)} async-done(((bf16[32,32,512]{2,1,0:T(8,128)(2,1)}), bf16[32,32,512]{2,1,0:T(8,128)(2,1)S(1)}, u32[]{:S(2)}, u32[]{:S(2)}) %all-to-all-start.9) | async-done | bytes 1048608 | tf_op jit(solution)/shard_map/all_to_all | solution.py:42
  437.3 14.7 %all_to_all.67 = f32[16,1,32]{2,1,0:T(1,128)S(1)} all-to-all(f32[16,1,32]{2,1,0:T(1,128)S(1)} %broadcast_in_dim.48), channel_id=1, replica_groups=mesh['band'=32,'seq'=16] {'seq'}, dimensions={0} | all-to-all | bytes 4096 | tf_op jit(solution)/shard_map/all_to_all | solution.py:34
  452.0 13.9 %all_to_all.68 = f32[32,1,32]{2,1,0:T(1,128)S(1)} all-to-all(f32[32,1,32]{2,1,0:T(1,128)S(1)} %broadcast_in_dim.49), channel_id=1, replica_groups=mesh['band'=32,'seq'=16] {'band'}, dimensions={0} | all-to-all | bytes 8192 | tf_op jit(solution)/shard_map/all_to_all | solution.py:34
  (123 shorter events, 49.6 us)
Async XLA Ops:
  57.8 8.5 %copy-start.3 = (s32[256]{0:T(256)S(1)}, s32[256]{0:T(256)}, u32[]{:S(2)}) copy-start(s32[256]{0:T(256)} %param.10) | copy-start | bytes 3076
  57.8 23.3 %copy-start.1 = (s32[4,32]{1,0:T(4,128)S(1)}, s32[4,32]{1,0:T(4,128)}, u32[]{:S(2)}) copy-start(s32[4,32]{1,0:T(4,128)} %param.12) | copy-start | bytes 1540
  57.8 24.1 %copy-start.2 = (s32[4,32]{1,0:T(4,128)S(1)}, s32[4,32]{1,0:T(4,128)}, u32[]{:S(2)}) copy-start(s32[4,32]{1,0:T(4,128)} %param.13) | copy-start | bytes 1540
  57.8 192.2 %all-to-all-start.2 = ((bf16[32,512,256]{2,1,0:T(8,128)(2,1)}), bf16[32,512,256]{2,1,0:T(8,128)(2,1)}, u32[]{:S(2)}, u32[]{:S(2)}) async-start(bf16[32,512,256]{2,1,0:T(8,128)(2,1)} %stack.48), calls=%async_computation.2 | async-start | bytes 16777216 | tf_op jit(solution)/shard_map/all_to_all | solution.py:78
  250.0 10.0 %copy-start = (bf16[512,256]{1,0:T(8,128)(2,1)S(1)}, bf16[512,256]{1,0:T(8,128)(2,1)}, u32[]{:S(2)}) copy-start(bf16[512,256]{1,0:T(8,128)(2,1)} %param.11) | copy-start | bytes 786436
  267.7 20.4 %collective-permute-start = (bf16[32,64]{1,0:T(8,128)(2,1)S(1)}, bf16[32,64]{1,0:T(8,128)(2,1)S(1)}, u32[]{:S(2)}, u32[]{:S(2)}) collective-permute-start(bf16[32,64]{1,0:T(8,128)(2,1)S(1)} %get-tuple-element.41), channel_id=1, source_target_pairs={{0,1},{1,2},{2,3},{3,4},{4,5},{5,6},{6,7},{7,8},{8,9},{9,10},{10,1... | collective-permute-start | bytes 12296 | tf_op jit(solution)/shard_map/ppermute | solution.py:21
  273.9 14.3 %collective-permute-start.1 = (bf16[32,64]{1,0:T(8,128)(2,1)S(1)}, bf16[32,64]{1,0:T(8,128)(2,1)S(1)}, u32[]{:S(2)}, u32[]{:S(2)}) collective-permute-start(bf16[32,64]{1,0:T(8,128)(2,1)S(1)} %get-tuple-element.42), channel_id=1, source_target_pairs={{1,0},{2,1},{3,2},{4,3},{5,4},{6,5},{7,6},{8,7},{9,8},{10,9},{11,1... | collective-permute-start | bytes 12296 | tf_op jit(solution)/shard_map/ppermute | solution.py:23
  276.5 20.3 %all-to-all-start.3 = ((f32[32,1,512]{2,1,0:T(1,128)}), f32[32,1,512]{2,1,0:T(1,128)S(1)}, u32[]{:S(2)}, u32[]{:S(2)}) async-start(f32[32,1,512]{2,1,0:T(1,128)} %mul.397), calls=%async_computation.3 | async-start | bytes 131072 | tf_op jit(solution)/shard_map/all_to_all | solution.py:42
  337.7 28.5 %all-to-all-start.6 = ((bf16[32,32,512]{2,1,0:T(8,128)(2,1)}), bf16[32,32,512]{2,1,0:T(8,128)(2,1)S(1)}, u32[]{:S(2)}, u32[]{:S(2)}) async-start(bf16[32,32,512]{2,1,0:T(8,128)(2,1)} %broadcast_in_dim.44), calls=%async_computation.6 | async-start | bytes 2097152 | tf_op jit(solution)/shard_map/all_to_all | solution.py:42
  341.7 6.0 %collective-permute-start.2 = (bf16[32,64]{1,0:T(8,128)(2,1)S(1)}, bf16[32,64]{1,0:T(8,128)(2,1)S(1)}, u32[]{:S(2)}, u32[]{:S(2)}) collective-permute-start(bf16[32,64]{1,0:T(8,128)(2,1)S(1)} %get-tuple-element.35), channel_id=1, source_target_pairs={{0,1},{1,2},{2,3},{3,4},{4,5},{5,6},{6,7},{7,8},{8,9},{9,10},{10,1... | collective-permute-start | bytes 12296 | tf_op jit(solution)/shard_map/ppermute | solution.py:21
  345.7 5.3 %collective-permute-start.3 = (bf16[32,64]{1,0:T(8,128)(2,1)S(1)}, bf16[32,64]{1,0:T(8,128)(2,1)S(1)}, u32[]{:S(2)}, u32[]{:S(2)}) collective-permute-start(bf16[32,64]{1,0:T(8,128)(2,1)S(1)} %get-tuple-element.36), channel_id=1, source_target_pairs={{1,0},{2,1},{3,2},{4,3},{5,4},{6,5},{7,6},{8,7},{9,8},{10,9},{11,1... | collective-permute-start | bytes 12296 | tf_op jit(solution)/shard_map/ppermute | solution.py:23
  402.7 28.5 %all-to-all-start.9 = ((bf16[32,32,512]{2,1,0:T(8,128)(2,1)}), bf16[32,32,512]{2,1,0:T(8,128)(2,1)S(1)}, u32[]{:S(2)}, u32[]{:S(2)}) async-start(bf16[32,32,512]{2,1,0:T(8,128)(2,1)} %broadcast_in_dim.47), calls=%async_computation.9 | async-start | bytes 2097152 | tf_op jit(solution)/shard_map/all_to_all | solution.py:42
  406.7 6.0 %collective-permute-start.4 = (bf16[32,64]{1,0:T(8,128)(2,1)S(1)}, bf16[32,64]{1,0:T(8,128)(2,1)S(1)}, u32[]{:S(2)}, u32[]{:S(2)}) collective-permute-start(bf16[32,64]{1,0:T(8,128)(2,1)S(1)} %get-tuple-element.29), channel_id=1, source_target_pairs={{0,1},{1,2},{2,3},{3,4},{4,5},{5,6},{6,7},{7,8},{8,9},{9,10},{10,1... | collective-permute-start | bytes 12296 | tf_op jit(solution)/shard_map/ppermute | solution.py:21
  410.6 5.3 %collective-permute-start.5 = (bf16[32,64]{1,0:T(8,128)(2,1)S(1)}, bf16[32,64]{1,0:T(8,128)(2,1)S(1)}, u32[]{:S(2)}, u32[]{:S(2)}) collective-permute-start(bf16[32,64]{1,0:T(8,128)(2,1)S(1)} %get-tuple-element.30), channel_id=1, source_target_pairs={{1,0},{2,1},{3,2},{4,3},{5,4},{6,5},{7,6},{8,7},{9,8},{10,9},{11,1... | collective-permute-start | bytes 12296 | tf_op jit(solution)/shard_map/ppermute | solution.py:23
